TPU v7x, 128 devices: a whole 4x4x4 slice. The times are simulated.
128 devices in a mesh: row: 16 (over y_lo, x, core), col: 8 (over z, y_hi).
Axes of the slice: x: 4, y: 4 (y_hi: 2, y_lo: 2; y = y_hi * 2 + y_lo), z: 4, core: 2. Of those that a mesh axis runs over, the one named last changes fastest.
Arguments:
- gate_feats: bfloat16 [16, 8, 1024, 256], P('row', 'col'), may hold values from -6 to 6
- adjacency: int32 [16, 8, 8, 5, 128, 128], P('row', 'col'), may hold values 0 or 1
- gate_count: int32 [16, 8], P('row', 'col'), may hold values from 128 to 1024, as said below
- membership: int32 [16, 8, 512, 1024], P('row', 'col'), may hold values 0 or 1
- tok_count: int32 [16, 8], P('row', 'col'), may hold values from 64 to 512, as said below
- w_msg: bfloat16 [256, 256], replicated, may hold values from -0.375 to 0.375
- w_query: bfloat16 [256, 256], replicated, may hold values from -0.375 to 0.375
- w_key: bfloat16 [256, 256], replicated, may hold values from -0.375 to 0.375
- w_value: bfloat16 [256, 256], replicated, may hold values from -0.375 to 0.375
- w_out: bfloat16 [256, 256], replicated, may hold values from -0.375 to 0.375
- w_score: bfloat16 [256], replicated, may hold values from -0.375 to 0.375
- cotangent: float32 [16, 8, 512], P('row', 'col'), may hold values from -6 to 6
Outputs:
- value_out: float32 [16, 8, 512], P('row', 'col')
- g_msg: float32 [256, 256], replicated
- g_query: float32 [256, 256], replicated
- g_key: float32 [256, 256], replicated
- g_value: float32 [256, 256], replicated
- g_out: float32 [256, 256], replicated
- g_score: float32 [256], replicated
Inputs may be any that keep to these rules, and one draw needn't show every extreme that they name: `gate_count`: some tile is full in every draw. `tok_count`: some tile is full in every draw.
All inputs are finite; a program needn't handle non-finite values. No bound on the sum of `adjacency` or of `membership` on one device may be relied on, other than what follows from the above.
Results may differ from a plain program's by a relative error of at most 0.017.
Values may be sent and summed in bfloat16 or wider, within the bound.
No kernel may reach another device: no remote copies, remote signals or barrier semaphores. Data moves between devices by JAX's collectives and lax.ppermute only.
A program may use at most 128 MiB of HBM per device.

v0:
```python
import math
import jax
import jax.numpy as jnp
from jax import lax
from jax.sharding import PartitionSpec as P

H = 256
HEADS = 2
HD = 128
BLK = 128
NB = 8
NT = 512
EPS = 1e-06


def with_halo(array, sides, width):
    for axis, dim in sides:
        size, length = (lax.axis_size(axis), array.shape[dim])
        up = [(i, (i + 1) % size) for i in range(size - 1)]
        down = [(j, i) for i, j in up]
        last = lax.slice_in_dim(array, length - width, length, axis=dim)
        first = lax.slice_in_dim(array, 0, width, axis=dim)
        before = lax.ppermute(last, axis, up)
        after = lax.ppermute(first, axis, down)
        array = jnp.concatenate([before, array, after], axis=dim)
    return array


def silu_grad(preact):
    sigmoid_val = jax.nn.sigmoid(preact)
    return sigmoid_val * (1.0 + preact * (1.0 - sigmoid_val))


def rms_forward(values_in):
    rscale = lax.rsqrt(jnp.mean(values_in * values_in, axis=-1, keepdims=True) + EPS)
    return (values_in * rscale, rscale)


def rms_backward(grad_in, normed, rscale):
    return rscale * (grad_in - normed * jnp.mean(grad_in * normed, axis=-1, keepdims=True))


def split_heads(rows_in):
    return rows_in.reshape(rows_in.shape[0], HEADS, HD)


def score_probs(query_rows, key_rows):
    scores = jnp.einsum(
        "qhd,khd->hqk",
        split_heads(query_rows),
        split_heads(key_rows),
        preferred_element_type=jnp.float32,
    )
    return jax.nn.sigmoid(scores / math.sqrt(HD) - math.log(NT))


def attend_sum(query_rows, key_rows, value_rows):
    weights = score_probs(query_rows, key_rows).astype(jnp.bfloat16)
    output = jnp.einsum(
        "hqk,khd->qhd", weights, split_heads(value_rows), preferred_element_type=jnp.float32
    )
    return output.reshape(query_rows.shape[0], H)


def score_grads(query_rows, grad_rows, key_rows, value_rows):
    probs_val = score_probs(query_rows, key_rows)
    grad_prob = jnp.einsum(
        "qhd,khd->hqk",
        split_heads(grad_rows),
        split_heads(value_rows),
        preferred_element_type=jnp.float32,
    )
    grad_score = (grad_prob * probs_val * (1.0 - probs_val) / math.sqrt(HD)).astype(jnp.bfloat16)
    return (probs_val.astype(jnp.bfloat16), grad_score)


def query_grad(query_rows, grad_rows, key_rows, value_rows):
    weights, grad_score = score_grads(query_rows, grad_rows, key_rows, value_rows)
    grad_query = jnp.einsum(
        "hqk,khd->qhd", grad_score, split_heads(key_rows), preferred_element_type=jnp.float32
    )
    return grad_query.reshape(query_rows.shape[0], H)


def key_value_grads(query_rows, grad_rows, key_rows, value_rows):
    weights, grad_score = score_grads(query_rows, grad_rows, key_rows, value_rows)
    grad_key = jnp.einsum(
        "hqk,qhd->khd", grad_score, split_heads(query_rows), preferred_element_type=jnp.float32
    )
    grad_val = jnp.einsum(
        "hqk,qhd->khd", weights, split_heads(grad_rows), preferred_element_type=jnp.float32
    )
    return jnp.concatenate(
        [grad_key.reshape(key_rows.shape[0], H), grad_val.reshape(key_rows.shape[0], H)], axis=1
    )


def project(rows_in, weight_mat):
    return jnp.dot(rows_in, weight_mat, preferred_element_type=jnp.float32).astype(jnp.bfloat16)


def body(
    gate_feats,
    adjacency,
    gate_count,
    membership,
    tok_count,
    w_msg,
    w_query,
    w_key,
    w_value,
    w_out,
    w_score,
    cotangent,
):
    gate_total = gate_feats.shape[2]
    gate_live = (jnp.arange(gate_total) < gate_count[0, 0]).astype(jnp.float32)
    live_feats = (gate_feats[0, 0].astype(jnp.float32) * gate_live[:, None]).astype(jnp.bfloat16)
    padded = with_halo(live_feats[None, None], (("row", 0), ("col", 1)), 1)
    sources = jnp.stack(
        [padded[1, 1], padded[0, 1], padded[2, 1], padded[1, 0], padded[1, 2]], axis=0
    )
    sources = sources.reshape(5, NB, BLK, H)
    adj_tiles = adjacency[0, 0]
    aggregate = jnp.einsum(
        "bkij,kbjh->bih",
        adj_tiles.astype(jnp.bfloat16),
        sources,
        preferred_element_type=jnp.float32,
    )
    degree = jnp.sum(adj_tiles, axis=(1, 3)).astype(jnp.float32)
    message = (aggregate / (degree[:, :, None] + 1.0)).astype(jnp.bfloat16).reshape(gate_total, H)
    preact = jnp.dot(message, w_msg, preferred_element_type=jnp.float32)
    hidden = (gate_live[:, None] * (live_feats.astype(jnp.float32) + jax.nn.silu(preact))).astype(
        jnp.bfloat16
    )
    member_rows = membership[0, 0].astype(jnp.bfloat16)
    member_count = jnp.sum(membership[0, 0], axis=1).astype(jnp.float32)[:, None]
    pooled = jnp.dot(member_rows, hidden, preferred_element_type=jnp.float32) / (member_count + 1.0)
    normed, rscale = rms_forward(pooled)
    token_live = (jnp.arange(NT) < tok_count[0, 0]).astype(jnp.float32)[:, None]
    tokens = (token_live * normed).astype(jnp.bfloat16)
    query_own = project(tokens, w_query)
    zero_rows = jnp.zeros((NT, H), jnp.float32)
    key_own = project(tokens, w_key)
    value_own = project(tokens, w_value)
    attended = attend_sum(
        query_own,
        lax.all_gather(key_own, "col", axis=0, tiled=True),
        lax.all_gather(value_own, "col", axis=0, tiled=True),
    )
    attended = attended.astype(jnp.bfloat16)
    proj = jnp.dot(attended, w_out, preferred_element_type=jnp.float32)
    pnormed, pscale = rms_forward(proj)
    mixed = tokens.astype(jnp.float32) + pnormed
    score_w = w_score.astype(jnp.float32)
    value_out = token_live[:, 0] * jnp.sum(mixed * score_w, axis=1)
    loss_weight = 1.0 / math.sqrt(lax.axis_size("row") * lax.axis_size("col") * NT)
    grad_value = token_live[:, 0] * cotangent[0, 0] * loss_weight
    g_score = jnp.sum(mixed * grad_value[:, None], axis=0)
    grad_mixed = grad_value[:, None] * score_w
    grad_proj = rms_backward(grad_mixed, pnormed, pscale).astype(jnp.bfloat16)
    g_out = jnp.einsum("nh,ne->he", attended, grad_proj, preferred_element_type=jnp.float32)
    grad_attn = jnp.dot(grad_proj, w_out.T, preferred_element_type=jnp.float32).astype(jnp.bfloat16)
    key_all, value_all = (
        lax.all_gather(key_own, "col", axis=0, tiled=True),
        lax.all_gather(value_own, "col", axis=0, tiled=True),
    )

    def add_query(running, pair_in):
        return (running + query_grad(query_own, grad_attn, pair_in[0], pair_in[1]), 0)

    grad_query, unused = lax.scan(
        add_query, zero_rows, (key_all.reshape(-1, NT, H), value_all.reshape(-1, NT, H))
    )
    key_part = key_all.reshape(lax.axis_size("col") * NT // NT, NT, H)
    value_part = value_all.reshape(lax.axis_size("col") * NT // NT, NT, H)
    terms = lax.map(
        lambda pair_in: key_value_grads(query_own, grad_attn, pair_in[0], pair_in[1]),
        (key_part, value_part),
    )
    key_sums = lax.psum_scatter(
        terms.reshape(lax.axis_size("col") * NT, 2 * H), "col", scatter_dimension=0, tiled=True
    )
    grad_query = grad_query.astype(jnp.bfloat16)
    grad_key = key_sums[:, :H].astype(jnp.bfloat16)
    grad_val = key_sums[:, H:].astype(jnp.bfloat16)
    g_query = jnp.einsum("nh,ne->he", tokens, grad_query, preferred_element_type=jnp.float32)
    g_key = jnp.einsum("nh,ne->he", tokens, grad_key, preferred_element_type=jnp.float32)
    g_value = jnp.einsum("nh,ne->he", tokens, grad_val, preferred_element_type=jnp.float32)
    grad_tokens = grad_mixed + jnp.dot(grad_query, w_query.T, preferred_element_type=jnp.float32)
    grad_tokens = grad_tokens + jnp.dot(grad_key, w_key.T, preferred_element_type=jnp.float32)
    grad_tokens = grad_tokens + jnp.dot(grad_val, w_value.T, preferred_element_type=jnp.float32)
    grad_pooled = rms_backward(token_live * grad_tokens, normed, rscale)
    grad_scaled = (grad_pooled / (member_count + 1.0)).astype(jnp.bfloat16)
    grad_hidden = jnp.einsum(
        "ng,nh->gh", member_rows, grad_scaled, preferred_element_type=jnp.float32
    )
    grad_pre = (gate_live[:, None] * grad_hidden * silu_grad(preact)).astype(jnp.bfloat16)
    g_msg = jnp.einsum("gh,ge->he", message, grad_pre, preferred_element_type=jnp.float32)
    summed = lax.psum((g_msg, g_query, g_key, g_value, g_out, g_score), ("row", "col"))
    return (value_out[None, None], summed[0], summed[1], summed[2], summed[3], summed[4], summed[5])


def solution(mesh):
    placed = (
        P("row", "col", None, None),
        P("row", "col", None, None, None, None),
        P("row", "col"),
        P("row", "col", None, None),
        P("row", "col"),
        P(),
        P(),
        P(),
        P(),
        P(),
        P(),
        P("row", "col", None),
    )
    return jax.shard_map(
        body,
        mesh=mesh,
        in_specs=placed,
        out_specs=(P("row", "col", None), P(), P(), P(), P(), P(), P()),
        check_vma=False,
    )
```

profile of v0, /device:TPU:1, one launch (start us, length us, event | category | flops | bytes accessed | tf_op | source)
XLA Modules:
  0.0 574.1 jit_solution(18341425830394711041)
XLA Ops:
  7.9 1.4 multiply_convert_fusion.3
  9.3 4.5 collective-permute-start
  13.9 1.9 collective-permute-start.1
  15.8 4.2 collective-permute-done
  20.0 4.4 collective-permute-done.1
  24.4 1.3 pad_maximum_fusion
  25.7 6.1 %collective-permute-start.2 = (bf16[3,1,1024,256]{3,2,1,0:T(8,128)(2,1)}, bf16[3,1,1024,256]{3,2,1,0:T(8,128)(2,1)}, u32[]{:S(2)}, u32[]{:S(2)}) collective-permute-start(bf16[3,1,1024,256]{3,2,1,0:T(8,128)(2,1)} %pad_maximum_fusion), channel_id=1, source_target_pairs={{0,1},{1,2},{2,3},{3,4},{4,5},{5,6},{6,7},{8,9},{9,10},{10,11},{11... | collective-permute-start | bytes 4718600 | tf_op jit(solution)/shard_map/ppermute | solution.py:23
  31.8 1.3 collective-permute-start.3
  33.3 1.8 reduce_sum.75
  37.2 21.7 %collective-permute-done.2 = bf16[3,1,1024,256]{3,2,1,0:T(8,128)(2,1)} collective-permute-done((bf16[3,1,1024,256]{3,2,1,0:T(8,128)(2,1)}, bf16[3,1,1024,256]{3,2,1,0:T(8,128)(2,1)}, u32[]{:S(2)}, u32[]{:S(2)}) %collective-permute-start.2) | collective-permute-done | bytes 1572896 | tf_op jit(solution)/shard_map/ppermute | solution.py:23
  60.1 34.4 %collective-permute-done.3 = bf16[3,1,1024,256]{3,2,1,0:T(8,128)(2,1)} collective-permute-done((bf16[3,1,1024,256]{3,2,1,0:T(8,128)(2,1)}, bf16[3,1,1024,256]{3,2,1,0:T(8,128)(2,1)}, u32[]{:S(2)}, u32[]{:S(2)}) %collective-permute-start.3) | collective-permute-done | bytes 1572896 | tf_op jit(solution)/shard_map/ppermute | solution.py:24
  101.8 58.7 %all-gather.3.cloned.1.call-done = bf16[4096,256]{1,0:T(8,128)(2,1)} async-done(((bf16[512,256]{1,0:T(8,128)(2,1)}), bf16[4096,256]{1,0:T(8,128)(2,1)}) %all-gather.3.cloned.1.call-update) | async-done | bytes 2097168 | tf_op jit(solution)/shard_map/all_gather | solution.py:150
  160.5 2.9 copy.43
  163.4 51.9 %all-gather.5.cloned.1.call-done = bf16[4096,256]{1,0:T(8,128)(2,1)} async-done(((bf16[512,256]{1,0:T(8,128)(2,1)}), bf16[4096,256]{1,0:T(8,128)(2,1)}) %all-gather.5.cloned.1.call-update) | async-done | bytes 2097168 | tf_op jit(solution)/shard_map/all_gather | solution.py:149
  215.4 4.2 copy.44
  219.5 9.6 %fusion.32 = bf16[2,128,512]{2,1,0:T(8,128)(2,1)} fusion(bf16[4096,2,128]{0,2,1:T(8,128)(2,1)S(1)} %bitcast.190, bf16[512,2,128]{0,2,1:T(8,128)(2,1)S(1)} %bitcast.182, bf16[4096,2,128]{0,2,1:T(8,128)(2,1)} %bitcast.191), kind=kOutput, calls=%fused_computation.49 | convolution fusion | flops 2172780544 | bytes 4718592 | tf_op jit(solution)/shard_map/hqk,khd->qhd/dot_general | solution.py:59
  229.2 1.4 multiply_reduce_fusion.2
  230.6 1.6 multiply_reduce_fusion
  232.7 1.8 convolution_convert_fusion
  235.6 2.4 copy.30
  238.0 52.7 %while.25 = (s32[]{:T(128)}, f32[8,512,512]{2,1,0:T(8,128)}, bf16[8,512,256]{2,1,0:T(8,128)(2,1)}, bf16[512,256]{0,1:T(8,128)(2,1)S(1)}, bf16[8,512,256]{1,2,0:T...) while((s32[]{:T(128)}, f32[8,512,512]{2,1,0:T(8,128)}, bf16[8,512,256]{2,1,0:T(8,128)(2,1)}, ...), condition=%wide.region_9.10_spmd, body=%wide.region_8.9_spmd.sunk | while | flops 542900224 | bytes 18875020 | solution.py:178
  240.9 1.7 fusion.152
  247.5 1.7 fusion.152
  254.1 1.7 fusion.152
  260.6 1.7 fusion.152
  267.2 1.7 fusion.152
  273.8 1.7 fusion.152
  280.4 1.7 fusion.152
  286.9 1.7 fusion.152
  289.5 1.1 constant_dynamic-update-slice_fusion.6
  291.8 53.8 %while.26 = (s32[]{:T(128)}, f32[512,256]{0,1:T(8,128)S(1)}, bf16[8,512,256]{1,2,0:T(8,128)(2,1)}, bf16[8,512,256]{2,1,0:T(8,128)(2,1)}, bf16[512,256]{1,0:T(8,1...) while((s32[]{:T(128)}, f32[512,256]{0,1:T(8,128)S(1)}, ...), condition=%wide.region_7.8_spmd.clone, body=%wide.region_6.7_spmd.clone.sunk | while | flops 408158208 | bytes 9437287 | solution.py:173
  294.4 1.7 constant_dynamic-slice_fusion.10
  296.1 2.3 fusion.160
  301.1 1.7 constant_dynamic-slice_fusion.10
  302.8 2.3 fusion.160
  306.3 1.1 copy.74
  307.8 1.7 constant_dynamic-slice_fusion.10
  309.5 2.3 fusion.160
  314.5 1.7 constant_dynamic-slice_fusion.10
  316.2 2.3 fusion.160
  319.7 1.1 copy.74
  321.3 1.7 constant_dynamic-slice_fusion.10
  322.9 2.3 fusion.160
  326.5 1.1 copy.74
  328.0 1.7 constant_dynamic-slice_fusion.10
  329.7 2.3 fusion.160
  333.3 1.1 copy.74
  334.8 1.7 constant_dynamic-slice_fusion.10
  336.5 2.3 fusion.160
  340.0 1.1 copy.74
  341.5 1.7 constant_dynamic-slice_fusion.10
  343.2 2.3 fusion.160
  346.6 2.1 fusion.91
  348.8 53.9 %reduce-scatter.2.cloned.1.call-done = f32[512,512]{1,0:T(8,128)} async-done(((f32[4096,512]{1,0:T(8,128)}), f32[512,512]{1,0:T(8,128)}) %reduce-scatter.2.cloned.1.call-update) | async-done | bytes 1048592 | tf_op jit(solution)/shard_map/reduce_scatter | solution.py:182
  402.7 1.3 convert.6
  405.9 1.3 fusion.74
  407.6 1.1 fusion.49
  408.7 3.2 fusion.28
  412.0 65.1 %psum.47 = f32[256]{0:T(256)} all-reduce(f32[256]{0:T(256)S(1)} %copy-done.29), channel_id=1, replica_groups=mesh['row'=16,'col'=8] {'row','col'}, use_global_device_ids=true, to_apply=%region_18.19 | all-reduce | flops 256 | bytes 2048 | tf_op jit(solution)/shard_map/psum | solution.py:201
  477.6 82.6 %all-reduce.3.cloned.1.call-done = (f32[256,256]{1,0:T(8,128)}, f32[256,256]{1,0:T(8,128)}, f32[256,256]{1,0:T(8,128)}, f32[256,256]{1,0:T(8,128)}, f32[256,256]{1,0:T(8,128)}) async-done(((f32[256,256]{1,0:T(8,128)}, f32[256,256]{1,0:T(8,128)}, f32[256,256]{1,0:T(8,128)}, f32[256,256]{1,0:T(8,128)}, f32[256,256]{1,0:T(8,128)}), (f32[256,256]{1,0:T(8,128)}, f32[256,256]{1,0:T(8,128)}, f32[256,256]{1,0:T(8,128)}, ...) | async-done | bytes 1310736 | tf_op jit(solution)/shard_map/psum | solution.py:201
  560.2 1.7 copy.99
  561.9 1.7 copy.100
  563.6 1.7 copy.101
  565.2 1.7 copy.102
  (238 shorter events, 70.9 us)
Async XLA Ops:
  7.2 222.0 %copy-start = (bf16[256,256]{1,0:T(8,128)(2,1)S(1)}, bf16[256,256]{1,0:T(8,128)(2,1)}, u32[]{:S(2)}) copy-start(bf16[256,256]{1,0:T(8,128)(2,1)} %param.25) | copy-start | bytes 393220
  7.2 153.3 %all-gather.3.cloned.1.call-start = ((), (), s32[]{:S(2)}) async-start(), calls=%async_computation.1 | async-start | bytes 2359296 | tf_op jit(solution)/shard_map/all_gather | solution.py:150
  7.9 88.9 %copy-start.24 = (f32[1024]{0:T(1024)}, f32[1024]{0:T(1024)S(1)}, u32[]{:S(2)}) copy-start(f32[1024]{0:T(1024)S(1)} %fusion.84) | copy-start | bytes 12292
  7.9 25.2 %copy-start.7 = (s32[1,1,8,5,128,128]{5,4,3,2,1,0:T(8,128)S(1)}, s32[1,1,8,5,128,128]{5,4,3,2,1,0:T(8,128)}, u32[]{:S(2)}) copy-start(s32[1,1,8,5,128,128]{5,4,3,2,1,0:T(8,128)} %param.17) | copy-start | bytes 7864324
  9.3 10.6 %collective-permute-start = (bf16[1,1,1024,256]{3,2,1,0:T(8,128)(2,1)S(1)}, bf16[1,1,1024,256]{3,2,1,0:T(8,128)(2,1)S(1)}, u32[]{:S(2)}, u32[]{:S(2)}) collective-permute-start(bf16[1,1,1024,256]{3,2,1,0:T(8,128)(2,1)S(1)} %multiply_convert_fusion.3), channel_id=1, source_target_pairs={{0,8},{8,16},{16,24},{24,32},{32,40},{40,48},{48,56},{56,64},{64,7... | collective-permute-start | bytes 1572872 | tf_op jit(solution)/shard_map/ppermute | solution.py:23
  13.9 10.5 %collective-permute-start.1 = (bf16[1,1,1024,256]{3,2,1,0:T(8,128)(2,1)S(1)}, bf16[1,1,1024,256]{3,2,1,0:T(8,128)(2,1)S(1)}, u32[]{:S(2)}, u32[]{:S(2)}) collective-permute-start(bf16[1,1,1024,256]{3,2,1,0:T(8,128)(2,1)S(1)} %multiply_convert_fusion.3), channel_id=1, source_target_pairs={{8,0},{16,8},{24,16},{32,24},{40,32},{48,40},{56,48},{64,56},{72,6... | collective-permute-start | bytes 1572872 | tf_op jit(solution)/shard_map/ppermute | solution.py:24
  20.0 4.4 copy-start.12
  24.4 1.3 copy-start.13
  25.7 10.2 %copy-start.10 = (bf16[1,1,1024,256]{3,2,1,0:T(8,128)(2,1)S(1)}, bf16[1,1,1024,256]{3,2,1,0:T(8,128)(2,1)}, u32[]{:S(2)}) copy-start(bf16[1,1,1024,256]{3,2,1,0:T(8,128)(2,1)} %param.16) | copy-start | bytes 1572868
  25.7 33.2 %collective-permute-start.2 = (bf16[3,1,1024,256]{3,2,1,0:T(8,128)(2,1)}, bf16[3,1,1024,256]{3,2,1,0:T(8,128)(2,1)}, u32[]{:S(2)}, u32[]{:S(2)}) collective-permute-start(bf16[3,1,1024,256]{3,2,1,0:T(8,128)(2,1)} %pad_maximum_fusion), channel_id=1, source_target_pairs={{0,1},{1,2},{2,3},{3,4},{4,5},{5,6},{6,7},{8,9},{9,10},{10,11},{11... | collective-permute-start | bytes 4718600 | tf_op jit(solution)/shard_map/ppermute | solution.py:23
  31.8 62.7 %collective-permute-start.3 = (bf16[3,1,1024,256]{3,2,1,0:T(8,128)(2,1)}, bf16[3,1,1024,256]{3,2,1,0:T(8,128)(2,1)}, u32[]{:S(2)}, u32[]{:S(2)}) collective-permute-start(bf16[3,1,1024,256]{3,2,1,0:T(8,128)(2,1)} %pad_maximum_fusion), channel_id=1, source_target_pairs={{1,0},{2,1},{3,2},{4,3},{5,4},{6,5},{7,6},{9,8},{10,9},{11,10},{12... | collective-permute-start | bytes 4718600 | tf_op jit(solution)/shard_map/ppermute | solution.py:24
  35.1 2.1 copy-start.14
  35.9 61.0 %copy-start.31 = (f32[512]{0:T(512)}, f32[512]{0:T(512)S(1)}, u32[]{:S(2)}) copy-start(f32[512]{0:T(512)S(1)} %convert_add_fusion.2) | copy-start | bytes 6148
  95.6 0.9 copy-start.23
  95.6 1.7 copy-start.8
  95.6 1.9 copy-start.11
  96.3 2.1 copy-start.21
  97.6 1.0 copy-start.15
  97.6 1.1 copy-start.16
  97.6 2.2 copy-start.17
  98.6 132.0 %copy-start.4 = (f32[256,512]{1,0:T(8,128)}, f32[256,512]{1,0:T(8,128)S(1)}, u32[]{:S(2)}) copy-start(f32[256,512]{1,0:T(8,128)S(1)} %get-tuple-element.241) | copy-start | bytes 1572868
  98.6 2.4 copy-start.33
  98.6 3.0 copy-start.30
  98.6 3.0 copy-start.19
  99.7 115.7 %all-gather.5.cloned.1.call-start = ((), (), s32[]{:S(2)}) async-start(), calls=%async_computation.2 | async-start | bytes 2359296 | tf_op jit(solution)/shard_map/all_gather | solution.py:149
  100.7 302.0 %reduce-scatter.2.cloned.1.call-start = ((), (), s32[]{:S(2)}) async-start(), calls=%async_computation.3 | async-start | bytes 9437184 | tf_op jit(solution)/shard_map/reduce_scatter | solution.py:182
  229.1 6.4 %copy-start.3 = (bf16[4096,256]{1,0:T(8,128)(2,1)S(1)}, bf16[4096,256]{1,0:T(8,128)(2,1)}, u32[]{:S(2)}) copy-start(bf16[4096,256]{1,0:T(8,128)(2,1)} %all-gather.5.cloned.1.call-done) | copy-start | bytes 6291460
  230.5 1.6 copy-start.6
  232.1 0.6 copy-start.28
  238.0 1.8 copy-start.1
  243.2 1.4 copy-start.2
  244.6 1.8 copy-start.1
  249.8 1.4 copy-start.2
  251.2 1.8 copy-start.1
  256.3 1.4 copy-start.2
  257.7 1.8 copy-start.1
  262.9 1.4 copy-start.2
  264.3 1.8 copy-start.1
  269.5 1.4 copy-start.2
  270.9 1.8 copy-start.1
  276.0 1.4 copy-start.2
  277.5 1.8 copy-start.1
  282.6 1.4 copy-start.2
  284.0 1.8 copy-start.1
  289.2 1.5 copy-start.2
  290.7 269.5 %all-reduce.3.cloned.1.call-start = ((), (), s32[]{:S(2)}) async-start(), calls=%async_computation.4 | async-start | bytes 2621440 | tf_op jit(solution)/shard_map/psum | solution.py:201
  348.8 58.7 %copy-start.5 = (f32[256,512]{1,0:T(8,128)S(1)}, f32[256,512]{1,0:T(8,128)}, u32[]{:S(2)}) copy-start(f32[256,512]{1,0:T(8,128)} %copy-done.4) | copy-start | bytes 1572868
  348.8 58.7 %copy-start.26 = (f32[256]{0:T(256)S(1)}, f32[256]{0:T(256)}, u32[]{:S(2)}) copy-start(f32[256]{0:T(256)} %convert_element_type.188) | copy-start | bytes 3076
  402.7 4.5 copy-start.18
  402.7 4.8 copy-start.20
  405.9 2.7 copy-start.9
  405.9 2.7 copy-start.25
  405.9 2.7 copy-start.32
  408.7 3.3 copy-start.29
  408.7 68.3 %copy-start.27 = (f32[512]{0:T(512)S(1)}, f32[512]{0:T(512)}, u32[]{:S(2)}) copy-start(f32[512]{0:T(512)} %get-tuple-element.209) | copy-start | bytes 6148
  560.2 6.7 %copy-start.22 = (f32[256,256]{1,0:T(8,128)S(1)}, f32[256,256]{1,0:T(8,128)}, u32[]{:S(2)}) copy-start(f32[256,256]{1,0:T(8,128)} %get-tuple-element.370) | copy-start | bytes 786436
Sparse Core Ops, SparseCore 0:
  99.8 60.6 all-gather.2
  163.4 51.8 all-gather.4
  290.8 111.8 reduce-scatter.1
  412.1 148.0 all-reduce.2
where the time goes:
time: 577 us; the launch traced here: 574 us
  waiting for transfers between devices  312 us (54%)
  local copies, waits for them, and re-layouts  82.6 us (14%)
  matrix products  72.8 us (13%)
  blocking collectives  65.1 us (11%)
  between operations  15.6 us (3%)
  starting transfers between devices  14.4 us (2%)
  other arithmetic  10.9 us (2%)
    psum x1, waiting for transfers between devices, body(): lax.psum((g_msg, g_query, g_key, g_value, g_out, g_score), ('row', 'col'))  82.6 us
    psum x1, blocking collectives, body(): lax.psum((g_msg, g_query, g_key, g_value, g_out, g_score), ('row', 'col'))  65.1 us
    all_gather x1, waiting for transfers between devices, body(): lax.all_gather(value_own, 'col', axis=0, tiled=True)  58.7 us
    reduce_scatter x1, waiting for transfers between devices, body(): lax.psum_scatter(terms.reshape(lax.axis_size('col') * NT, 2 * H), 'col',...  53.9 us
    all_gather x1, waiting for transfers between devices, body(): lax.all_gather(key_own, 'col', axis=0, tiled=True)  51.9 us
    ppermute x2, waiting for transfers between devices, with_halo(): after = lax.ppermute(first, axis, down)  38.8 us
    dynamic_slice x32, local copies, waits for them, and re-layouts, body(): lax.scan(add_query, zero_rows, (key_all.reshape(-1, NT, H), value_all.res...  37.6 us
    ppermute x2, waiting for transfers between devices, with_halo(): before = lax.ppermute(last, axis, up)  25.9 us
  transfers between devices with their start and end apart: 8, of which 8 were waited for; matrix products, arithmetic and copies ran while one was open for 12% of the time, Pallas kernels for 0%

commit v1 on v0

--- a/solution.py
+++ b/solution.py
@@ -198,7 +198,8 @@
     )
     grad_pre = (gate_live[:, None] * grad_hidden * silu_grad(preact)).astype(jnp.bfloat16)
     g_msg = jnp.einsum("gh,ge->he", message, grad_pre, preferred_element_type=jnp.float32)
-    summed = lax.psum((g_msg, g_query, g_key, g_value, g_out, g_score), ("row", "col"))
+    one_axis = lax.psum((g_msg, g_query, g_key, g_value, g_out, g_score), "col")
+    summed = lax.psum(one_axis, "row")
     return (value_out[None, None], summed[0], summed[1], summed[2], summed[3], summed[4], summed[5])
 
 

time: 577 us -> 643 us (1.11)
  waiting for transfers between devices: 312 us -> 390 us
  blocking collectives: 65.1 us -> 53.5 us
    psum x1 -> x2, waiting for transfers between devices: 82.6 us -> 161 us  [the longest x1 88.7 us: body(): one_axis = lax.psum((g_msg, g_query, g_key, g_value, g_out, g_score), 'col')]
    psum x1 -> x2, blocking collectives: 65.1 us -> 53.5 us  [the longest x1 35 us: body(): summed = lax.psum(one_axis, 'row')]
  transfers between devices with their start and end apart: 8 -> 9, of which waited for: 8 -> 9; matrix products, arithmetic and copies ran while one was open for 12% -> 11% of each run, Pallas kernels for 0% -> 0%
where the time goes in v1:
time: 643 us; the launch traced here: 641 us
  waiting for transfers between devices  390 us (61%)
  local copies, waits for them, and re-layouts  82.5 us (13%)
  matrix products  72.9 us (11%)
  blocking collectives  53.5 us (8%)
  between operations  15.6 us (2%)
  starting transfers between devices  14.4 us (2%)
  other arithmetic  10.9 us (2%)
    psum x1, waiting for transfers between devices, body(): one_axis = lax.psum((g_msg, g_query, g_key, g_value, g_out, g_score), 'col')  88.7 us
    psum x1, waiting for transfers between devices, body(): summed = lax.psum(one_axis, 'row')  72.1 us
    all_gather x1, waiting for transfers between devices, body(): lax.all_gather(value_own, 'col', axis=0, tiled=True)  58.7 us
    reduce_scatter x1, waiting for transfers between devices, body(): lax.psum_scatter(terms.reshape(lax.axis_size('col') * NT, 2 * H), 'col',...  53.8 us
    all_gather x1, waiting for transfers between devices, body(): lax.all_gather(key_own, 'col', axis=0, tiled=True)  51.9 us
    ppermute x2, waiting for transfers between devices, with_halo(): after = lax.ppermute(first, axis, down)  38.8 us
    dynamic_slice x32, local copies, waits for them, and re-layouts, body(): lax.scan(add_query, zero_rows, (key_all.reshape(-1, NT, H), value_all.res...  37.5 us
    psum x1, blocking collectives, body(): summed = lax.psum(one_axis, 'row')  35 us
  transfers between devices with their start and end apart: 9, of which 9 were waited for; matrix products, arithmetic and copies ran while one was open for 11% of the time, Pallas kernels for 0%

profile of v1, /device:TPU:1, one launch (start us, length us, event | category | flops | bytes accessed | tf_op | source)
XLA Modules:
  0.0 640.9 jit_solution(5606768925575048924)
XLA Ops:
  7.9 1.4 multiply_convert_fusion.3
  9.3 4.5 collective-permute-start
  13.9 1.9 collective-permute-start.1
  15.8 4.2 collective-permute-done
  20.0 4.4 collective-permute-done.1
  24.4 1.3 pad_maximum_fusion
  25.7 6.1 collective-permute-start.2
  31.8 1.3 collective-permute-start.3
  33.3 1.8 reduce_sum.75
  37.2 21.7 %collective-permute-done.2 = bf16[3,1,1024,256]{3,2,1,0:T(8,128)(2,1)} collective-permute-done((bf16[3,1,1024,256]{3,2,1,0:T(8,128)(2,1)}, bf16[3,1,1024,256]{3,2,1,0:T(8,128)(2,1)}, u32[]{:S(2)}, u32[]{:S(2)}) %collective-permute-start.2) | collective-permute-done | bytes 1572896 | tf_op jit(solution)/shard_map/ppermute | solution.py:23
  60.1 34.4 %collective-permute-done.3 = bf16[3,1,1024,256]{3,2,1,0:T(8,128)(2,1)} collective-permute-done((bf16[3,1,1024,256]{3,2,1,0:T(8,128)(2,1)}, bf16[3,1,1024,256]{3,2,1,0:T(8,128)(2,1)}, u32[]{:S(2)}, u32[]{:S(2)}) %collective-permute-start.3) | collective-permute-done | bytes 1572896 | tf_op jit(solution)/shard_map/ppermute | solution.py:24
  101.8 58.7 %all-gather.3.cloned.1.call-done = bf16[4096,256]{1,0:T(8,128)(2,1)} async-done(((bf16[512,256]{1,0:T(8,128)(2,1)}), bf16[4096,256]{1,0:T(8,128)(2,1)}) %all-gather.3.cloned.1.call-update) | async-done | bytes 2097168 | tf_op jit(solution)/shard_map/all_gather | solution.py:150
  160.5 2.9 copy.43
  163.4 51.9 %all-gather.5.cloned.1.call-done = bf16[4096,256]{1,0:T(8,128)(2,1)} async-done(((bf16[512,256]{1,0:T(8,128)(2,1)}), bf16[4096,256]{1,0:T(8,128)(2,1)}) %all-gather.5.cloned.1.call-update) | async-done | bytes 2097168 | tf_op jit(solution)/shard_map/all_gather | solution.py:149
  215.3 4.1 copy.44
  219.5 9.6 %fusion.32 = bf16[2,128,512]{2,1,0:T(8,128)(2,1)} fusion(bf16[4096,2,128]{0,2,1:T(8,128)(2,1)S(1)} %bitcast.190, bf16[512,2,128]{0,2,1:T(8,128)(2,1)S(1)} %bitcast.182, bf16[4096,2,128]{0,2,1:T(8,128)(2,1)} %bitcast.191), kind=kOutput, calls=%fused_computation.49 | convolution fusion | flops 2172780544 | bytes 4718592 | tf_op jit(solution)/shard_map/hqk,khd->qhd/dot_general | solution.py:59
  229.1 1.4 multiply_reduce_fusion.2
  230.5 1.6 multiply_reduce_fusion
  232.6 1.8 convolution_convert_fusion
  235.5 2.4 copy.30
  237.9 52.7 %while.25 = (s32[]{:T(128)}, f32[8,512,512]{2,1,0:T(8,128)}, bf16[8,512,256]{2,1,0:T(8,128)(2,1)}, bf16[512,256]{0,1:T(8,128)(2,1)S(1)}, bf16[8,512,256]{1,2,0:T...) while((s32[]{:T(128)}, f32[8,512,512]{2,1,0:T(8,128)}, bf16[8,512,256]{2,1,0:T(8,128)(2,1)}, ...), condition=%wide.region_9.10_spmd, body=%wide.region_8.9_spmd.sunk | while | flops 542900224 | bytes 18875020 | solution.py:178
  240.8 1.7 fusion.152
  247.4 1.7 fusion.152
  254.0 1.7 fusion.152
  260.5 1.7 fusion.152
  267.1 1.7 fusion.152
  273.7 1.7 fusion.152
  280.3 1.7 fusion.152
  286.8 1.7 fusion.152
  289.5 1.1 constant_dynamic-update-slice_fusion.6
  291.7 54.0 %while.26 = (s32[]{:T(128)}, f32[512,256]{0,1:T(8,128)S(1)}, bf16[8,512,256]{1,2,0:T(8,128)(2,1)}, bf16[8,512,256]{2,1,0:T(8,128)(2,1)}, bf16[512,256]{1,0:T(8,1...) while((s32[]{:T(128)}, f32[512,256]{0,1:T(8,128)S(1)}, ...), condition=%wide.region_7.8_spmd.clone, body=%wide.region_6.7_spmd.clone.sunk | while | flops 408158208 | bytes 9437287 | solution.py:173
  294.3 1.7 constant_dynamic-slice_fusion.10
  296.0 2.3 fusion.160
  301.1 1.7 constant_dynamic-slice_fusion.10
  302.7 2.3 fusion.160
  307.8 1.7 constant_dynamic-slice_fusion.10
  309.5 2.3 fusion.160
  314.5 1.7 constant_dynamic-slice_fusion.10
  316.2 2.3 fusion.160
  319.7 1.1 copy.74
  321.3 1.7 constant_dynamic-slice_fusion.10
  323.0 2.3 fusion.160
  328.1 1.7 constant_dynamic-slice_fusion.10
  329.7 2.3 fusion.160
  333.3 1.1 copy.74
  334.8 1.7 constant_dynamic-slice_fusion.10
  336.5 2.3 fusion.160
  340.1 1.1 copy.74
  341.6 1.7 constant_dynamic-slice_fusion.10
  343.3 2.3 fusion.160
  346.7 2.1 fusion.91
  348.9 53.8 %reduce-scatter.2.cloned.1.call-done = f32[512,512]{1,0:T(8,128)} async-done(((f32[4096,512]{1,0:T(8,128)}), f32[512,512]{1,0:T(8,128)}) %reduce-scatter.2.cloned.1.call-update) | async-done | bytes 1048592 | tf_op jit(solution)/shard_map/reduce_scatter | solution.py:182
  402.7 1.3 convert.6
  405.9 1.3 fusion.74
  407.5 1.1 fusion.49
  408.6 3.2 fusion.28
  411.9 88.7 %all-reduce.7.cloned.1.call-done = (f32[256,256]{1,0:T(8,128)}, f32[256,256]{1,0:T(8,128)}, f32[256,256]{1,0:T(8,128)}, f32[256,256]{1,0:T(8,128)}, f32[256,256]{1,0:T(8,128)}) async-done(((f32[256,256]{1,0:T(8,128)}, f32[256,256]{1,0:T(8,128)}, f32[256,256]{1,0:T(8,128)}, f32[256,256]{1,0:T(8,128)}, f32[256,256]{1,0:T(8,128)}), (f32[256,256]{1,0:T(8,128)}, f32[256,256]{1,0:T(8,128)}, f32[256,256]{1,0:T(8,128)}, ...) | async-done | bytes 1310736 | tf_op jit(solution)/shard_map/psum | solution.py:201
  500.7 18.5 %psum.94 = f32[256]{0:T(256)S(1)} all-reduce(f32[256]{0:T(256)S(1)} %copy-done.29), channel_id=1, replica_groups=mesh['row'=16,'col'=8] {'col'}, use_global_device_ids=true, to_apply=%region_23.24 | all-reduce | flops 256 | bytes 2048 | tf_op jit(solution)/shard_map/psum | solution.py:201
  519.1 35.0 %psum.95 = f32[256]{0:T(256)} all-reduce(f32[256]{0:T(256)S(1)} %psum.94), channel_id=1, replica_groups=mesh['row'=16,'col'=8] {'row'}, use_global_device_ids=true, to_apply=%region_24.25 | all-reduce | flops 256 | bytes 2048 | tf_op jit(solution)/shard_map/psum | solution.py:202
  554.7 72.1 %all-reduce.5.cloned.1.call-done = (f32[256,256]{1,0:T(8,128)}, f32[256,256]{1,0:T(8,128)}, f32[256,256]{1,0:T(8,128)}, f32[256,256]{1,0:T(8,128)}, f32[256,256]{1,0:T(8,128)}) async-done(((f32[256,256]{1,0:T(8,128)}, f32[256,256]{1,0:T(8,128)}, f32[256,256]{1,0:T(8,128)}, f32[256,256]{1,0:T(8,128)}, f32[256,256]{1,0:T(8,128)}), (f32[256,256]{1,0:T(8,128)}, f32[256,256]{1,0:T(8,128)}, f32[256,256]{1,0:T(8,128)}, ...) | async-done | bytes 1310736 | tf_op jit(solution)/shard_map/psum | solution.py:202
  626.9 1.7 copy.104
  628.6 1.7 copy.105
  630.3 1.7 copy.106
  631.9 1.7 copy.107
  (242 shorter events, 73.1 us)
Async XLA Ops:
  7.2 221.9 %copy-start = (bf16[256,256]{1,0:T(8,128)(2,1)S(1)}, bf16[256,256]{1,0:T(8,128)(2,1)}, u32[]{:S(2)}) copy-start(bf16[256,256]{1,0:T(8,128)(2,1)} %param.25) | copy-start | bytes 393220
  7.2 153.3 %all-gather.3.cloned.1.call-start = ((), (), s32[]{:S(2)}) async-start(), calls=%async_computation.1 | async-start | bytes 2359296 | tf_op jit(solution)/shard_map/all_gather | solution.py:150
  7.9 88.9 %copy-start.24 = (f32[1024]{0:T(1024)}, f32[1024]{0:T(1024)S(1)}, u32[]{:S(2)}) copy-start(f32[1024]{0:T(1024)S(1)} %fusion.84) | copy-start | bytes 12292
  7.9 25.2 %copy-start.7 = (s32[1,1,8,5,128,128]{5,4,3,2,1,0:T(8,128)S(1)}, s32[1,1,8,5,128,128]{5,4,3,2,1,0:T(8,128)}, u32[]{:S(2)}) copy-start(s32[1,1,8,5,128,128]{5,4,3,2,1,0:T(8,128)} %param.17) | copy-start | bytes 7864324
  9.3 10.6 %collective-permute-start = (bf16[1,1,1024,256]{3,2,1,0:T(8,128)(2,1)S(1)}, bf16[1,1,1024,256]{3,2,1,0:T(8,128)(2,1)S(1)}, u32[]{:S(2)}, u32[]{:S(2)}) collective-permute-start(bf16[1,1,1024,256]{3,2,1,0:T(8,128)(2,1)S(1)} %multiply_convert_fusion.3), channel_id=1, source_target_pairs={{0,8},{8,16},{16,24},{24,32},{32,40},{40,48},{48,56},{56,64},{64,7... | collective-permute-start | bytes 1572872 | tf_op jit(solution)/shard_map/ppermute | solution.py:23
  13.9 10.5 %collective-permute-start.1 = (bf16[1,1,1024,256]{3,2,1,0:T(8,128)(2,1)S(1)}, bf16[1,1,1024,256]{3,2,1,0:T(8,128)(2,1)S(1)}, u32[]{:S(2)}, u32[]{:S(2)}) collective-permute-start(bf16[1,1,1024,256]{3,2,1,0:T(8,128)(2,1)S(1)} %multiply_convert_fusion.3), channel_id=1, source_target_pairs={{8,0},{16,8},{24,16},{32,24},{40,32},{48,40},{56,48},{64,56},{72,6... | collective-permute-start | bytes 1572872 | tf_op jit(solution)/shard_map/ppermute | solution.py:24
  20.0 4.4 copy-start.12
  24.4 1.3 copy-start.13
  25.7 10.2 %copy-start.10 = (bf16[1,1,1024,256]{3,2,1,0:T(8,128)(2,1)S(1)}, bf16[1,1,1024,256]{3,2,1,0:T(8,128)(2,1)}, u32[]{:S(2)}) copy-start(bf16[1,1,1024,256]{3,2,1,0:T(8,128)(2,1)} %param.16) | copy-start | bytes 1572868
  25.7 33.2 %collective-permute-start.2 = (bf16[3,1,1024,256]{3,2,1,0:T(8,128)(2,1)}, bf16[3,1,1024,256]{3,2,1,0:T(8,128)(2,1)}, u32[]{:S(2)}, u32[]{:S(2)}) collective-permute-start(bf16[3,1,1024,256]{3,2,1,0:T(8,128)(2,1)} %pad_maximum_fusion), channel_id=1, source_target_pairs={{0,1},{1,2},{2,3},{3,4},{4,5},{5,6},{6,7},{8,9},{9,10},{10,11},{11... | collective-permute-start | bytes 4718600 | tf_op jit(solution)/shard_map/ppermute | solution.py:23
  31.8 62.7 %collective-permute-start.3 = (bf16[3,1,1024,256]{3,2,1,0:T(8,128)(2,1)}, bf16[3,1,1024,256]{3,2,1,0:T(8,128)(2,1)}, u32[]{:S(2)}, u32[]{:S(2)}) collective-permute-start(bf16[3,1,1024,256]{3,2,1,0:T(8,128)(2,1)} %pad_maximum_fusion), channel_id=1, source_target_pairs={{1,0},{2,1},{3,2},{4,3},{5,4},{6,5},{7,6},{9,8},{10,9},{11,10},{12... | collective-permute-start | bytes 4718600 | tf_op jit(solution)/shard_map/ppermute | solution.py:24
  35.1 2.1 copy-start.14
  35.8 61.0 %copy-start.31 = (f32[512]{0:T(512)}, f32[512]{0:T(512)S(1)}, u32[]{:S(2)}) copy-start(f32[512]{0:T(512)S(1)} %convert_add_fusion.2) | copy-start | bytes 6148
  95.6 0.9 copy-start.23
  95.6 1.7 copy-start.8
  95.6 1.9 copy-start.11
  96.3 2.1 copy-start.21
  97.6 1.0 copy-start.15
  97.6 1.1 copy-start.16
  97.6 2.1 copy-start.17
  98.5 131.9 %copy-start.4 = (f32[256,512]{1,0:T(8,128)}, f32[256,512]{1,0:T(8,128)S(1)}, u32[]{:S(2)}) copy-start(f32[256,512]{1,0:T(8,128)S(1)} %get-tuple-element.246) | copy-start | bytes 1572868
  98.5 2.4 copy-start.33
  98.6 3.0 copy-start.30
  98.6 3.0 copy-start.19
  99.6 115.7 %all-gather.5.cloned.1.call-start = ((), (), s32[]{:S(2)}) async-start(), calls=%async_computation.2 | async-start | bytes 2359296 | tf_op jit(solution)/shard_map/all_gather | solution.py:149
  100.7 301.9 %reduce-scatter.2.cloned.1.call-start = ((), (), s32[]{:S(2)}) async-start(), calls=%async_computation.3 | async-start | bytes 9437184 | tf_op jit(solution)/shard_map/reduce_scatter | solution.py:182
  229.1 6.4 %copy-start.3 = (bf16[4096,256]{1,0:T(8,128)(2,1)S(1)}, bf16[4096,256]{1,0:T(8,128)(2,1)}, u32[]{:S(2)}) copy-start(bf16[4096,256]{1,0:T(8,128)(2,1)} %all-gather.5.cloned.1.call-done) | copy-start | bytes 6291460
  230.5 1.6 copy-start.6
  232.0 0.6 copy-start.28
  237.9 1.8 copy-start.1
  243.1 1.4 copy-start.2
  244.5 1.8 copy-start.1
  249.7 1.4 copy-start.2
  251.1 1.8 copy-start.1
  256.2 1.4 copy-start.2
  257.6 1.8 copy-start.1
  262.8 1.4 copy-start.2
  264.2 1.8 copy-start.1
  269.4 1.4 copy-start.2
  270.8 1.8 copy-start.1
  276.0 1.4 copy-start.2
  277.4 1.8 copy-start.1
  282.6 1.4 copy-start.2
  284.0 1.8 copy-start.1
  289.1 1.5 copy-start.2
  290.6 210.0 %all-reduce.7.cloned.1.call-start = ((), (), s32[]{:S(2)}) async-start(), calls=%async_computation.5 | async-start | bytes 2621440 | tf_op jit(solution)/shard_map/psum | solution.py:201
  348.9 58.6 %copy-start.5 = (f32[256,512]{1,0:T(8,128)S(1)}, f32[256,512]{1,0:T(8,128)}, u32[]{:S(2)}) copy-start(f32[256,512]{1,0:T(8,128)} %copy-done.4) | copy-start | bytes 1572868
  348.9 58.6 %copy-start.26 = (f32[256]{0:T(256)S(1)}, f32[256]{0:T(256)}, u32[]{:S(2)}) copy-start(f32[256]{0:T(256)} %convert_element_type.188) | copy-start | bytes 3076
  402.7 4.5 copy-start.18
  402.7 4.8 copy-start.20
  405.9 2.7 copy-start.9
  405.9 2.7 copy-start.25
  405.9 2.7 copy-start.32
  411.9 88.8 %copy-start.29 = (f32[256]{0:T(256)S(1)}, f32[256]{0:T(256)}, u32[]{:S(2)}) copy-start(f32[256]{0:T(256)} %get-tuple-element.208) | copy-start | bytes 3076
  411.9 142.3 %copy-start.27 = (f32[512]{0:T(512)S(1)}, f32[512]{0:T(512)}, u32[]{:S(2)}) copy-start(f32[512]{0:T(512)} %get-tuple-element.209) | copy-start | bytes 6148
  411.9 215.0 %all-reduce.5.cloned.1.call-start = ((), (), s32[]{:S(2)}) async-start(), calls=%async_computation.4 | async-start | bytes 2621440 | tf_op jit(solution)/shard_map/psum | solution.py:202
  626.9 6.7 %copy-start.22 = (f32[256,256]{1,0:T(8,128)S(1)}, f32[256,256]{1,0:T(8,128)}, u32[]{:S(2)}) copy-start(f32[256,256]{1,0:T(8,128)} %get-tuple-element.375) | copy-start | bytes 786436
Sparse Core Ops, SparseCore 0:
  99.8 60.6 all-gather.2
  163.4 51.8 all-gather.4
  290.7 111.8 reduce-scatter.1
  412.0 88.5 all-reduce.6
  503.6 123.2 all-reduce.4
